TPU v7x, 512 devices: a whole 4x8x8 slice. The times are simulated.
512 devices in a mesh: seq: 64 (over z, y), chan: 8 (over x, core).
Axes of the slice: x: 4, y: 8, z: 8, core: 2. Of those that a mesh axis runs over, the one named last changes fastest.
Arguments:
- tokens: bfloat16 [8192, 4096], P('seq', 'chan'), may hold values from -6 to 6
- conv_taps: float32 [4, 4096], P(None, 'chan'), may hold values from -12 to 12
- log_rate: float32 [4096], P('chan'), may hold values from 4.8828125e-06 to 0.034
- rotation: float32 [4096], P('chan'), may hold values from 0 to 0.2
- in_proj: bfloat16 [64, 64, 128], P('chan'), may hold values from -0.75 to 0.75
- out_proj: bfloat16 [64, 64, 128], P('chan'), may hold values from -0.5 to 0.5
- skip_gain: float32 [4096], P('chan'), may hold values from 0.25 to 1.5
- norm_gain: float32 [4096], P('chan'), may hold values from 0.25 to 1.75
- retention: float32 [8192], P('seq'), may hold values from 0.5 to 1
- cotangent: bfloat16 [8192, 4096], P('seq', 'chan'), may hold values from -6 to 6
Outputs:
- normed: bfloat16 [8192, 4096], P('seq', 'chan')
- tokens_grad: bfloat16 [8192, 4096], P('seq', 'chan')
- in_grad: float32 [64, 64, 128], P('chan')
- out_grad: float32 [64, 64, 128], P('chan')
- taps_grad: float32 [4, 4096], P(None, 'chan')
All inputs are finite; a program needn't handle non-finite values.
Results may differ from a plain program's by a relative error of at most 0.011.
Values may be sent and summed in bfloat16 or wider, within the bound.
No kernel may reach another device: no remote copies, remote signals or barrier semaphores. Data moves between devices by JAX's collectives and lax.ppermute only.
A program may use at most 64 MiB of HBM per device.

v0:
```python
import jax
import jax.numpy as jnp
from jax import lax
from jax.sharding import Mesh, PartitionSpec as P

SEQ = ("z", "y")


def from_behind(value, axis, by):
    length = lax.axis_size(axis)
    pairs = [(i, i + by) for i in range(length) if 0 <= i + by < length]
    return lax.ppermute(value, axis, pairs)


def carried_in(part, axis, combine, identity, reverse):
    count = lax.axis_size(axis)
    place = lax.axis_index(axis)
    ahead = count - 1 - place if reverse else place
    step = -1 if reverse else 1
    packed = jnp.stack(part)
    unit = jnp.stack([jnp.zeros_like(a) + jnp.asarray(e, a.dtype) for a, e in zip(part, identity)])
    state = jnp.where(ahead >= 1, from_behind(packed, axis, step), unit)
    reach = 1
    while reach < count:
        earlier = from_behind(state, axis, step * reach)
        joined = jnp.stack(combine(tuple(earlier), tuple(state)))
        state = jnp.where(ahead >= reach, joined, state)
        reach *= 2
    return tuple(state)


def linear_run(drive_re, drive_im, decay_rate, turn_rate, log_keep):
    seq_len, num_cols = drive_re.shape
    block_len = min(64, seq_len)
    block_count = seq_len // block_len
    offsets = jnp.arange(block_len, dtype=jnp.float32)
    keep_cum = jnp.cumsum(log_keep.reshape(block_count, block_len), axis=1)[:, :, None]
    angles = offsets[:, None] * turn_rate[None, :]
    cosine = jnp.cos(angles)
    sine = jnp.sin(angles)
    growth = jnp.exp(offsets[None, :, None] * decay_rate[None, None, :] - keep_cum)
    blk_re = drive_re.reshape(block_count, block_len, num_cols)
    blk_im = drive_im.reshape(block_count, block_len, num_cols)
    pre_re = growth * (blk_re * cosine + blk_im * sine)
    pre_im = growth * (blk_im * cosine - blk_re * sine)
    lower_ones = (offsets[:, None] >= offsets[None, :]).astype(jnp.float32)
    summed = jnp.einsum(
        "ji,abik->abjk", lower_ones, jnp.stack([pre_re, pre_im]), precision=lax.Precision.HIGHEST
    )
    shrink = jnp.exp(keep_cum - offsets[None, :, None] * decay_rate[None, None, :])
    state_re = shrink * (summed[0] * cosine - summed[1] * sine)
    state_im = shrink * (summed[0] * sine + summed[1] * cosine)
    step_mag = jnp.exp(keep_cum[:, -1] - block_len * decay_rate[None, :])
    step_re = step_mag * jnp.cos(block_len * turn_rate)[None, :]
    step_im = step_mag * jnp.sin(block_len * turn_rate)[None, :]

    def advance(carried, inputs):
        carry_re, carry_im = carried
        mult_re, mult_im, end_re, end_im = inputs
        next_re = mult_re * carry_re - mult_im * carry_im + end_re
        next_im = mult_re * carry_im + mult_im * carry_re + end_im
        return ((next_re, next_im), (carry_re, carry_im))

    zeros_col = jnp.zeros((num_cols,), jnp.float32)
    enter_re, enter_im = lax.scan(
        advance, (zeros_col, zeros_col), (step_re, step_im, state_re[:, -1], state_im[:, -1])
    )[1]
    ahead = offsets + 1.0
    lift = jnp.exp(keep_cum - ahead[None, :, None] * decay_rate[None, None, :])
    lift_re = lift * jnp.cos(ahead[:, None] * turn_rate[None, :])
    lift_im = lift * jnp.sin(ahead[:, None] * turn_rate[None, :])
    state_re = state_re + lift_re * enter_re[:, None] - lift_im * enter_im[:, None]
    state_im = state_im + lift_re * enter_im[:, None] + lift_im * enter_re[:, None]
    return (state_re.reshape(seq_len, num_cols), state_im.reshape(seq_len, num_cols))


def carry_combine(earlier, later):
    early_re, early_im, early_sre, early_sim = earlier
    late_re, late_im, late_sre, late_sim = later
    joined_re = early_re * late_re - early_im * late_im
    joined_im = early_re * late_im + early_im * late_re
    joined_sre = late_re * early_sre - late_im * early_sim + late_sre
    joined_sim = late_re * early_sim + late_im * early_sre + late_sim
    return (joined_re, joined_im, joined_sre, joined_sim)


def per_device(
    tokens,
    conv_taps,
    log_rate,
    rotation,
    in_proj,
    out_proj,
    skip_gain,
    norm_gain,
    retention,
    cotangent,
):
    seq_len, local_width = tokens.shape
    tap_count = conv_taps.shape[0]
    local_heads, head_width, double_state = in_proj.shape
    state_size = double_state // 2
    num_cols = local_heads * state_size
    lead_rows = from_behind(tokens[seq_len - (tap_count - 1) :], SEQ, 1)
    padded = jnp.concatenate([lead_rows, tokens], axis=0).astype(jnp.float32)
    conv_sum = conv_taps[0][None, :] * padded[tap_count - 1 :]
    for offset in range(1, tap_count):
        conv_sum = (
            conv_sum
            + conv_taps[offset][None, :]
            * padded[tap_count - 1 - offset : tap_count - 1 - offset + seq_len]
        )
    mixed_in = conv_sum.astype(jnp.bfloat16)
    by_head = mixed_in.reshape(seq_len, local_heads, head_width)
    projected = jnp.einsum("thc,hck->thk", by_head, in_proj, preferred_element_type=jnp.float32)
    in_scale = jnp.sqrt(-jnp.expm1(-2.0 * log_rate))
    drive_re = projected[:, :, :state_size].reshape(seq_len, num_cols) * in_scale
    drive_im = projected[:, :, state_size:].reshape(seq_len, num_cols) * in_scale
    log_keep = jnp.log(retention)
    state_re, state_im = linear_run(drive_re, drive_im, log_rate, rotation, log_keep)
    keep_total = jnp.sum(log_keep)
    total_mag = jnp.exp(keep_total - seq_len * log_rate)
    total_re = total_mag * jnp.cos(seq_len * rotation)
    total_im = total_mag * jnp.sin(seq_len * rotation)
    unit_ones = jnp.ones((num_cols,), jnp.float32)
    zeros_col = jnp.zeros((num_cols,), jnp.float32)
    chained = carried_in(
        (total_re, total_im, state_re[-1], state_im[-1]),
        SEQ,
        carry_combine,
        (unit_ones, zeros_col, zeros_col, zeros_col),
        False,
    )
    enter_re, enter_im = (chained[2], chained[3])
    positions = jnp.arange(seq_len, dtype=jnp.float32)
    ahead = positions + 1.0
    lift = jnp.exp(jnp.cumsum(log_keep)[:, None] - ahead[:, None] * log_rate[None, :])
    lift_re = lift * jnp.cos(ahead[:, None] * rotation[None, :])
    lift_im = lift * jnp.sin(ahead[:, None] * rotation[None, :])
    state_re = state_re + lift_re * enter_re[None, :] - lift_im * enter_im[None, :]
    state_im = state_im + lift_re * enter_im[None, :] + lift_im * enter_re[None, :]
    state_bf = jnp.concatenate(
        [
            state_re.reshape(seq_len, local_heads, state_size),
            state_im.reshape(seq_len, local_heads, state_size),
        ],
        axis=2,
    ).astype(jnp.bfloat16)
    mixed = jnp.einsum(
        "thk,hck->thc", state_bf, out_proj, preferred_element_type=jnp.float32
    ).reshape(seq_len, local_width)
    mixed = mixed + skip_gain * mixed_in.astype(jnp.float32)
    squares = jnp.sum(mixed * mixed, axis=1)
    scaled = cotangent.astype(jnp.float32) * norm_gain
    dots = jnp.sum(scaled * mixed, axis=1)
    squares = lax.psum(squares, "chan")
    model_width = local_width * lax.axis_size("chan")
    inverse = lax.rsqrt(squares / model_width + 1e-06)
    normed = (mixed * inverse[:, None] * norm_gain).astype(jnp.bfloat16)
    dots = lax.psum(dots, "chan")
    mixed_grad = inverse[:, None] * (
        scaled - mixed * (inverse * inverse * dots / model_width)[:, None]
    )
    grad_bf = mixed_grad.astype(jnp.bfloat16).reshape(seq_len, local_heads, head_width)
    state_grad = jnp.einsum("thc,hck->thk", grad_bf, out_proj, preferred_element_type=jnp.float32)
    out_grad = jnp.einsum("thc,thk->hck", grad_bf, state_bf, preferred_element_type=jnp.float32)
    out_grad = lax.psum(lax.psum(out_grad, "y"), "z")
    back_keep = jnp.concatenate([jnp.zeros((1,), jnp.float32), log_keep[::-1][:-1]])
    grad_re = state_grad[:, :, :state_size].reshape(seq_len, num_cols)[::-1]
    grad_im = state_grad[:, :, state_size:].reshape(seq_len, num_cols)[::-1]
    adj_re, adj_im = linear_run(grad_re, grad_im, log_rate, -rotation, back_keep)
    first_mag = jnp.exp(log_keep[0] - log_rate)
    cos_turn = jnp.cos(rotation)
    sin_turn = jnp.sin(rotation)
    first_re = first_mag * (cos_turn * adj_re[-1] + sin_turn * adj_im[-1])
    first_im = first_mag * (cos_turn * adj_im[-1] - sin_turn * adj_re[-1])
    back_chained = carried_in(
        (total_re, -total_im, first_re, first_im),
        SEQ,
        carry_combine,
        (unit_ones, zeros_col, zeros_col, zeros_col),
        True,
    )
    later_re, later_im = (back_chained[2], back_chained[3])
    back_lift = jnp.exp(jnp.cumsum(back_keep)[:, None] - positions[:, None] * log_rate[None, :])
    back_re = back_lift * jnp.cos(positions[:, None] * rotation[None, :])
    back_im = -back_lift * jnp.sin(positions[:, None] * rotation[None, :])
    adj_re = adj_re + back_re * later_re[None, :] - back_im * later_im[None, :]
    adj_im = adj_im + back_re * later_im[None, :] + back_im * later_re[None, :]
    adj_re = adj_re[::-1]
    adj_im = adj_im[::-1]
    drive_grad = jnp.concatenate(
        [
            (in_scale * adj_re).reshape(seq_len, local_heads, state_size),
            (in_scale * adj_im).reshape(seq_len, local_heads, state_size),
        ],
        axis=2,
    ).astype(jnp.bfloat16)
    in_grad = jnp.einsum("thc,thk->hck", by_head, drive_grad, preferred_element_type=jnp.float32)
    input_grad = jnp.einsum(
        "thk,hck->thc", drive_grad, in_proj, preferred_element_type=jnp.float32
    ).reshape(seq_len, local_width)
    input_grad = input_grad + skip_gain * mixed_grad
    trail_rows = from_behind(input_grad[: tap_count - 1], SEQ, -1)
    tail = jnp.concatenate([input_grad, trail_rows], axis=0)
    tokens_grad = conv_taps[0][None, :] * tail[:seq_len]
    for offset in range(1, tap_count):
        tokens_grad = tokens_grad + conv_taps[offset][None, :] * tail[offset : offset + seq_len]
    taps_grad = jnp.stack(
        [
            jnp.sum(
                input_grad * padded[tap_count - 1 - offset : tap_count - 1 - offset + seq_len],
                axis=0,
            )
            for offset in range(tap_count)
        ]
    )
    packed = jnp.concatenate([in_grad.reshape(-1), taps_grad.reshape(-1)])
    packed = lax.psum(lax.psum(packed, "y"), "z")
    in_grad = packed[: in_grad.size].reshape(in_grad.shape)
    taps_grad = packed[in_grad.size :].reshape(taps_grad.shape)
    return (normed, tokens_grad.astype(jnp.bfloat16), in_grad, out_grad, taps_grad)


def solution(mesh):
    seq_count, chan_count = mesh.devices.shape
    inner = 1
    while inner * inner < seq_count:
        inner *= 2
    devices = mesh.devices.reshape(seq_count // inner, inner, chan_count)
    mesh = Mesh(devices, SEQ + ("chan",))
    in_specs = (
        P(SEQ, "chan"),
        P(None, "chan"),
        P("chan"),
        P("chan"),
        P("chan", None, None),
        P("chan", None, None),
        P("chan"),
        P("chan"),
        P(SEQ),
        P(SEQ, "chan"),
    )
    out_specs = (
        P(SEQ, "chan"),
        P(SEQ, "chan"),
        P("chan", None, None),
        P("chan", None, None),
        P(None, "chan"),
    )
    return jax.shard_map(
        per_device, mesh=mesh, in_specs=in_specs, out_specs=out_specs, check_vma=False
    )
```

profile of v0, /device:TPU:2, one launch (start us, length us, event | category | flops | bytes accessed | tf_op | source)
XLA Modules:
  0.0 364.7 jit_solution(13326804845153230500)
XLA Ops:
  8.2 3.5 collective-permute-start
  14.9 1.3 fusion.68
  16.2 2.5 multiply_cosine_fusion.1
  21.0 1.0 fusion.18
  27.2 3.5 collective-permute-start.1
  30.7 1.3 collective-permute-done.1
  32.1 4.2 %collective-permute-start.2 = (f32[4,512]{1,0:T(4,128)S(1)}, f32[4,512]{1,0:T(4,128)S(1)}, u32[]{:S(2)}, u32[]{:S(2)}) collective-permute-start(f32[4,512]{1,0:T(4,128)S(1)} %broadcast_select_fusion.5), channel_id=1, source_target_pairs={{0,8},{8,16},{16,24},{24,32},{32,40},{40,48},{48,56},{56,64},{64,7... | collective-permute-start | bytes 24584 | tf_op jit(solution)/shard_map/ppermute | solution.py:12
  36.2 1.3 collective-permute-done.2
  37.6 5.7 %collective-permute-start.3 = (f32[4,512]{1,0:T(4,128)S(1)}, f32[4,512]{1,0:T(4,128)S(1)}, u32[]{:S(2)}, u32[]{:S(2)}) collective-permute-start(f32[4,512]{1,0:T(4,128)S(1)} %maximum_select_fusion), channel_id=1, source_target_pairs={{0,16},{8,24},{16,32},{24,40},{32,48},{40,56},{48,64},{56,72},{64,... | collective-permute-start | bytes 24584 | tf_op jit(solution)/shard_map/ppermute | solution.py:12
  43.4 1.3 collective-permute-done.3
  44.8 10.6 %collective-permute-start.4 = (f32[4,512]{1,0:T(4,128)S(1)}, f32[4,512]{1,0:T(4,128)S(1)}, u32[]{:S(2)}, u32[]{:S(2)}) collective-permute-start(f32[4,512]{1,0:T(4,128)S(1)} %maximum_select_fusion.1), channel_id=1, source_target_pairs={{0,32},{8,40},{16,48},{24,56},{32,64},{40,72},{48,80},{56,88},{64,... | collective-permute-start | bytes 24584 | tf_op jit(solution)/shard_map/ppermute | solution.py:12
  55.4 1.3 collective-permute-done.4
  56.8 9.1 %collective-permute-start.5 = (f32[4,512]{1,0:T(4,128)S(1)}, f32[4,512]{1,0:T(4,128)S(1)}, u32[]{:S(2)}, u32[]{:S(2)}) collective-permute-start(f32[4,512]{1,0:T(4,128)S(1)} %maximum_select_fusion.2), channel_id=1, source_target_pairs={{0,64},{8,72},{16,80},{24,88},{32,96},{40,104},{48,112},{56,120},{... | collective-permute-start | bytes 24584 | tf_op jit(solution)/shard_map/ppermute | solution.py:12
  65.9 1.3 collective-permute-done.5
  67.4 6.1 %collective-permute-start.6 = (f32[4,512]{1,0:T(4,128)S(1)}, f32[4,512]{1,0:T(4,128)S(1)}, u32[]{:S(2)}, u32[]{:S(2)}) collective-permute-start(f32[4,512]{1,0:T(4,128)S(1)} %maximum_select_fusion.3), channel_id=1, source_target_pairs={{0,128},{8,136},{16,144},{24,152},{32,160},{40,168},{48,176},{56,1... | collective-permute-start | bytes 24584 | tf_op jit(solution)/shard_map/ppermute | solution.py:12
  73.5 1.3 collective-permute-done.6
  76.1 17.7 %collective-permute-start.7 = (f32[4,512]{1,0:T(4,128)}, f32[4,512]{1,0:T(4,128)}, u32[]{:S(2)}, u32[]{:S(2)}) collective-permute-start(f32[4,512]{1,0:T(4,128)} %maximum_select_fusion.4), channel_id=1, source_target_pairs={{0,256},{8,264},{16,272},{24,280},{32,288},{40,296},{48,304},{56,3... | collective-permute-start | bytes 24584 | tf_op jit(solution)/shard_map/ppermute | solution.py:12
  97.4 1.1 sub.357
  99.4 0.9 copy.136
  100.3 0.9 copy.138
  102.5 0.9 copy.140
  108.8 1.1 squeeze.79
  109.9 0.9 copy.141
  111.7 0.9 copy.135
  113.0 0.9 multiply_subtract_fusion.7
  115.5 2.7 subtract_convert_fusion
  119.7 10.2 %all-reduce = (f32[128]{0:T(128)S(1)}, f32[128]{0:T(128)S(1)}) all-reduce(f32[128]{0:T(128)S(1)} %get-tuple-element.185, f32[128]{0:T(128)S(1)} %get-tuple-element.184), channel_id=1, replica_groups=mesh['z'=8,'y'=8,'chan'=8] {'chan'}, use_global_device_ids=true, to_apply=%region_6.7 | all-reduce | flops 256 | bytes 2048 | tf_op jit(solution)/shard_map/psum | solution.py:156
  137.2 1.3 collective-permute-start.8
  138.5 4.2 %collective-permute-done.8 = f32[4,512]{1,0:T(4,128)S(1)} collective-permute-done((f32[4,512]{1,0:T(4,128)S(1)}, f32[4,512]{1,0:T(4,128)S(1)}, u32[]{:S(2)}, u32[]{:S(2)}) %collective-permute-start.8) | collective-permute-done | bytes 8224 | tf_op jit(solution)/shard_map/ppermute | solution.py:12
  142.7 1.3 collective-permute-start.9
  144.0 4.2 %collective-permute-done.9 = f32[4,512]{1,0:T(4,128)S(1)} collective-permute-done((f32[4,512]{1,0:T(4,128)S(1)}, f32[4,512]{1,0:T(4,128)S(1)}, u32[]{:S(2)}, u32[]{:S(2)}) %collective-permute-start.9) | collective-permute-done | bytes 8224 | tf_op jit(solution)/shard_map/ppermute | solution.py:12
  148.3 1.3 collective-permute-start.10
  149.6 5.1 %collective-permute-done.10 = f32[4,512]{1,0:T(4,128)S(1)} collective-permute-done((f32[4,512]{1,0:T(4,128)S(1)}, f32[4,512]{1,0:T(4,128)S(1)}, u32[]{:S(2)}, u32[]{:S(2)}) %collective-permute-start.10) | collective-permute-done | bytes 8224 | tf_op jit(solution)/shard_map/ppermute | solution.py:12
  154.8 1.3 collective-permute-start.11
  156.1 8.1 %collective-permute-done.11 = f32[4,512]{1,0:T(4,128)S(1)} collective-permute-done((f32[4,512]{1,0:T(4,128)S(1)}, f32[4,512]{1,0:T(4,128)S(1)}, u32[]{:S(2)}, u32[]{:S(2)}) %collective-permute-start.11) | collective-permute-done | bytes 8224 | tf_op jit(solution)/shard_map/ppermute | solution.py:12
  164.3 1.3 collective-permute-start.12
  165.6 4.3 %collective-permute-done.12 = f32[4,512]{1,0:T(4,128)S(1)} collective-permute-done((f32[4,512]{1,0:T(4,128)S(1)}, f32[4,512]{1,0:T(4,128)S(1)}, u32[]{:S(2)}, u32[]{:S(2)}) %collective-permute-start.12) | collective-permute-done | bytes 8224 | tf_op jit(solution)/shard_map/ppermute | solution.py:12
  170.0 1.3 collective-permute-start.13
  172.3 4.1 %collective-permute-done.13 = f32[4,512]{1,0:T(4,128)S(1)} collective-permute-done((f32[4,512]{1,0:T(4,128)S(1)}, f32[4,512]{1,0:T(4,128)S(1)}, u32[]{:S(2)}, u32[]{:S(2)}) %collective-permute-start.13) | collective-permute-done | bytes 8224 | tf_op jit(solution)/shard_map/ppermute | solution.py:12
  176.5 1.3 collective-permute-start.14
  177.8 1.0 fusion.35
  178.8 7.2 %collective-permute-done.14 = f32[4,512]{1,0:T(4,128)S(1)} collective-permute-done((f32[4,512]{1,0:T(4,128)S(1)}, f32[4,512]{1,0:T(4,128)S(1)}, u32[]{:S(2)}, u32[]{:S(2)}) %collective-permute-start.14) | collective-permute-done | bytes 8224 | tf_op jit(solution)/shard_map/ppermute | solution.py:12
  186.7 1.1 multiply_subtract_fusion
  192.1 80.6 %all-reduce.6.cloned.1.call-done = (f32[67584]{0:T(1024)}, f32[8,64,128]{2,1,0:T(8,128)}) async-done(((f32[67584]{0:T(1024)}, f32[8,64,128]{2,1,0:T(8,128)}), (f32[67584]{0:T(1024)}, f32[8,64,128]{2,1,0:T(8,128)})) %all-reduce.6.cloned.1.call-update) | async-done | bytes 532496 | tf_op jit(solution)/shard_map/psum | solution.py:219
  272.7 1.3 collective-permute-start.15
  274.8 6.2 %collective-permute-done.15 = f32[3,512]{0,1:T(8,128)S(1)} collective-permute-done((f32[3,512]{0,1:T(8,128)S(1)}, f32[3,512]{0,1:T(8,128)S(1)}, u32[]{:S(2)}, u32[]{:S(2)}) %collective-permute-start.15) | collective-permute-done | bytes 6176 | tf_op jit(solution)/shard_map/ppermute | solution.py:12
  282.5 71.6 %all-reduce.8.cloned.1.call-done = (f32[67584]{0:T(1024)}, f32[8,64,128]{2,1,0:T(8,128)}) async-done(((f32[67584]{0:T(1024)}, f32[8,64,128]{2,1,0:T(8,128)}), (f32[67584]{0:T(1024)}, f32[8,64,128]{2,1,0:T(8,128)})) %all-reduce.8.cloned.1.call-update) | async-done | bytes 532496 | tf_op jit(solution)/shard_map/psum | solution.py:219
  354.1 1.7 slice.228
  (359 shorter events, 45.8 us)
Async XLA Ops:
  7.2 111.1 %copy-start = (bf16[8,64,128]{2,1,0:T(8,128)(2,1)S(1)}, bf16[8,64,128]{2,1,0:T(8,128)(2,1)}, u32[]{:S(2)}) copy-start(bf16[8,64,128]{2,1,0:T(8,128)(2,1)} %param.19) | copy-start | bytes 393220
  7.2 265.5 %all-reduce.6.cloned.1.call-start = ((), (), s32[]{:S(2)}) async-start(), calls=%async_computation | async-start | bytes 1064960 | tf_op jit(solution)/shard_map/psum | solution.py:219
  8.1 3.5 copy-start.88
  8.2 13.9 %collective-permute-start = (bf16[3,512]{0,1:T(8,128)(2,1)S(1)}, bf16[3,512]{0,1:T(8,128)(2,1)S(1)}, u32[]{:S(2)}, u32[]{:S(2)}) collective-permute-start(bf16[3,512]{0,1:T(8,128)(2,1)S(1)} %copy.131), channel_id=1, source_target_pairs={{0,8},{8,16},{16,24},{24,32},{32,40},{40,48},{48,56},{56,64},{64,7... | collective-permute-start | bytes 9224 | tf_op jit(solution)/shard_map/ppermute | solution.py:12
  14.2 81.8 %copy-start.72 = (f32[2,64]{1,0:T(2,128)}, f32[2,64]{1,0:T(2,128)S(1)}, u32[]{:S(2)}) copy-start(f32[2,64]{1,0:T(2,128)S(1)} %reduce.6) | copy-start | bytes 1540
  16.2 8.3 %copy-start.57 = (f32[512]{0:T(512)}, f32[512]{0:T(512)S(1)}, u32[]{:S(2)}) copy-start(f32[512]{0:T(512)S(1)} %get-tuple-element.356) | copy-start | bytes 6148
  16.2 11.0 %copy-start.59 = (f32[512]{0:T(512)}, f32[512]{0:T(512)S(1)}, u32[]{:S(2)}) copy-start(f32[512]{0:T(512)S(1)} %get-tuple-element.352) | copy-start | bytes 6148
  18.7 1.5 copy-start.14
  20.2 2.0 copy-start.49
  20.3 2.0 copy-start.51
  20.3 2.0 copy-start.53
  20.3 2.0 copy-start.55
  27.2 4.8 %collective-permute-start.1 = (f32[4,512]{1,0:T(4,128)S(1)}, f32[4,512]{1,0:T(4,128)S(1)}, u32[]{:S(2)}, u32[]{:S(2)}) collective-permute-start(f32[4,512]{1,0:T(4,128)S(1)} %fusion.48), channel_id=1, source_target_pairs={{0,8},{8,16},{16,24},{24,32},{32,40},{40,48},{48,56},{56,64},{64,7... | collective-permute-start | bytes 24584 | tf_op jit(solution)/shard_map/ppermute | solution.py:12
  32.1 5.5 %collective-permute-start.2 = (f32[4,512]{1,0:T(4,128)S(1)}, f32[4,512]{1,0:T(4,128)S(1)}, u32[]{:S(2)}, u32[]{:S(2)}) collective-permute-start(f32[4,512]{1,0:T(4,128)S(1)} %broadcast_select_fusion.5), channel_id=1, source_target_pairs={{0,8},{8,16},{16,24},{24,32},{32,40},{40,48},{48,56},{56,64},{64,7... | collective-permute-start | bytes 24584 | tf_op jit(solution)/shard_map/ppermute | solution.py:12
  37.6 7.1 %collective-permute-start.3 = (f32[4,512]{1,0:T(4,128)S(1)}, f32[4,512]{1,0:T(4,128)S(1)}, u32[]{:S(2)}, u32[]{:S(2)}) collective-permute-start(f32[4,512]{1,0:T(4,128)S(1)} %maximum_select_fusion), channel_id=1, source_target_pairs={{0,16},{8,24},{16,32},{24,40},{32,48},{40,56},{48,64},{56,72},{64,... | collective-permute-start | bytes 24584 | tf_op jit(solution)/shard_map/ppermute | solution.py:12
  44.7 30.2 %copy-start.17 = (f32[1,512]{1,0:T(1,128)}, f32[1,512]{1,0:T(1,128)S(1)}, u32[]{:S(2)}) copy-start(f32[1,512]{1,0:T(1,128)S(1)} %get-tuple-element.319) | copy-start | bytes 6148
  44.7 30.2 %copy-start.19 = (f32[1,512]{1,0:T(1,128)}, f32[1,512]{1,0:T(1,128)S(1)}, u32[]{:S(2)}) copy-start(f32[1,512]{1,0:T(1,128)S(1)} %get-tuple-element.320) | copy-start | bytes 6148
  44.7 30.2 %copy-start.21 = (f32[1,512]{1,0:T(1,128)}, f32[1,512]{1,0:T(1,128)S(1)}, u32[]{:S(2)}) copy-start(f32[1,512]{1,0:T(1,128)S(1)} %get-tuple-element.321) | copy-start | bytes 6148
  44.8 30.2 %copy-start.23 = (f32[1,512]{1,0:T(1,128)}, f32[1,512]{1,0:T(1,128)S(1)}, u32[]{:S(2)}) copy-start(f32[1,512]{1,0:T(1,128)S(1)} %get-tuple-element.322) | copy-start | bytes 6148
  44.8 11.9 %collective-permute-start.4 = (f32[4,512]{1,0:T(4,128)S(1)}, f32[4,512]{1,0:T(4,128)S(1)}, u32[]{:S(2)}, u32[]{:S(2)}) collective-permute-start(f32[4,512]{1,0:T(4,128)S(1)} %maximum_select_fusion.1), channel_id=1, source_target_pairs={{0,32},{8,40},{16,48},{24,56},{32,64},{40,72},{48,80},{56,88},{64,... | collective-permute-start | bytes 24584 | tf_op jit(solution)/shard_map/ppermute | solution.py:12
  56.7 18.2 %copy-start.29 = (f32[1,512]{1,0:T(1,128)}, f32[1,512]{1,0:T(1,128)S(1)}, u32[]{:S(2)}) copy-start(f32[1,512]{1,0:T(1,128)S(1)} %get-tuple-element.315) | copy-start | bytes 6148
  56.7 18.2 %copy-start.31 = (f32[1,512]{1,0:T(1,128)}, f32[1,512]{1,0:T(1,128)S(1)}, u32[]{:S(2)}) copy-start(f32[1,512]{1,0:T(1,128)S(1)} %get-tuple-element.316) | copy-start | bytes 6148
  56.7 18.2 %copy-start.33 = (f32[1,512]{1,0:T(1,128)}, f32[1,512]{1,0:T(1,128)S(1)}, u32[]{:S(2)}) copy-start(f32[1,512]{1,0:T(1,128)S(1)} %get-tuple-element.317) | copy-start | bytes 6148
  56.8 18.2 %copy-start.35 = (f32[1,512]{1,0:T(1,128)}, f32[1,512]{1,0:T(1,128)S(1)}, u32[]{:S(2)}) copy-start(f32[1,512]{1,0:T(1,128)S(1)} %get-tuple-element.318) | copy-start | bytes 6148
  56.8 10.5 %collective-permute-start.5 = (f32[4,512]{1,0:T(4,128)S(1)}, f32[4,512]{1,0:T(4,128)S(1)}, u32[]{:S(2)}, u32[]{:S(2)}) collective-permute-start(f32[4,512]{1,0:T(4,128)S(1)} %maximum_select_fusion.2), channel_id=1, source_target_pairs={{0,64},{8,72},{16,80},{24,88},{32,96},{40,104},{48,112},{56,120},{... | collective-permute-start | bytes 24584 | tf_op jit(solution)/shard_map/ppermute | solution.py:12
  67.3 7.7 %copy-start.41 = (f32[1,512]{1,0:T(1,128)}, f32[1,512]{1,0:T(1,128)S(1)}, u32[]{:S(2)}) copy-start(f32[1,512]{1,0:T(1,128)S(1)} %get-tuple-element.311) | copy-start | bytes 6148
  67.3 7.7 %copy-start.43 = (f32[1,512]{1,0:T(1,128)}, f32[1,512]{1,0:T(1,128)S(1)}, u32[]{:S(2)}) copy-start(f32[1,512]{1,0:T(1,128)S(1)} %get-tuple-element.312) | copy-start | bytes 6148
  67.3 7.7 %copy-start.45 = (f32[1,512]{1,0:T(1,128)}, f32[1,512]{1,0:T(1,128)S(1)}, u32[]{:S(2)}) copy-start(f32[1,512]{1,0:T(1,128)S(1)} %get-tuple-element.313) | copy-start | bytes 6148
  67.3 7.7 %copy-start.47 = (f32[1,512]{1,0:T(1,128)}, f32[1,512]{1,0:T(1,128)S(1)}, u32[]{:S(2)}) copy-start(f32[1,512]{1,0:T(1,128)S(1)} %get-tuple-element.314) | copy-start | bytes 6148
  67.4 7.4 %collective-permute-start.6 = (f32[4,512]{1,0:T(4,128)S(1)}, f32[4,512]{1,0:T(4,128)S(1)}, u32[]{:S(2)}, u32[]{:S(2)}) collective-permute-start(f32[4,512]{1,0:T(4,128)S(1)} %maximum_select_fusion.3), channel_id=1, source_target_pairs={{0,128},{8,136},{16,144},{24,152},{32,160},{40,168},{48,176},{56,1... | collective-permute-start | bytes 24584 | tf_op jit(solution)/shard_map/ppermute | solution.py:12
  76.1 36.8 %collective-permute-start.7 = (f32[4,512]{1,0:T(4,128)}, f32[4,512]{1,0:T(4,128)}, u32[]{:S(2)}, u32[]{:S(2)}) collective-permute-start(f32[4,512]{1,0:T(4,128)} %maximum_select_fusion.4), channel_id=1, source_target_pairs={{0,256},{8,264},{16,272},{24,280},{32,288},{40,296},{48,304},{56,3... | collective-permute-start | bytes 24584 | tf_op jit(solution)/shard_map/ppermute | solution.py:12
  111.7 2.2 copy-start.68
  112.6 2.3 copy-start.6
  112.6 2.3 copy-start.7
  112.7 2.3 copy-start.8
  132.1 1.7 copy-start.38
  132.1 2.7 copy-start.11
  132.1 2.7 copy-start.12
  137.2 5.5 %collective-permute-start.8 = (f32[4,512]{1,0:T(4,128)S(1)}, f32[4,512]{1,0:T(4,128)S(1)}, u32[]{:S(2)}, u32[]{:S(2)}) collective-permute-start(f32[4,512]{1,0:T(4,128)S(1)} %fusion.50), channel_id=1, source_target_pairs={{8,0},{16,8},{24,16},{32,24},{40,32},{48,40},{56,48},{64,56},{72,6... | collective-permute-start | bytes 24584 | tf_op jit(solution)/shard_map/ppermute | solution.py:12
  142.7 5.5 %collective-permute-start.9 = (f32[4,512]{1,0:T(4,128)S(1)}, f32[4,512]{1,0:T(4,128)S(1)}, u32[]{:S(2)}, u32[]{:S(2)}) collective-permute-start(f32[4,512]{1,0:T(4,128)S(1)} %broadcast_select_fusion.4), channel_id=1, source_target_pairs={{8,0},{16,8},{24,16},{32,24},{40,32},{48,40},{56,48},{64,56},{72,6... | collective-permute-start | bytes 24584 | tf_op jit(solution)/shard_map/ppermute | solution.py:12
  148.3 6.4 %collective-permute-start.10 = (f32[4,512]{1,0:T(4,128)S(1)}, f32[4,512]{1,0:T(4,128)S(1)}, u32[]{:S(2)}, u32[]{:S(2)}) collective-permute-start(f32[4,512]{1,0:T(4,128)S(1)} %maximum_select_fusion.6), channel_id=1, source_target_pairs={{16,0},{24,8},{32,16},{40,24},{48,32},{56,40},{64,48},{72,56},{80,... | collective-permute-start | bytes 24584 | tf_op jit(solution)/shard_map/ppermute | solution.py:12
  154.8 9.5 %collective-permute-start.11 = (f32[4,512]{1,0:T(4,128)S(1)}, f32[4,512]{1,0:T(4,128)S(1)}, u32[]{:S(2)}, u32[]{:S(2)}) collective-permute-start(f32[4,512]{1,0:T(4,128)S(1)} %maximum_select_fusion.7), channel_id=1, source_target_pairs={{32,0},{40,8},{48,16},{56,24},{64,32},{72,40},{80,48},{88,56},{96,... | collective-permute-start | bytes 24584 | tf_op jit(solution)/shard_map/ppermute | solution.py:12
  164.3 5.6 %collective-permute-start.12 = (f32[4,512]{1,0:T(4,128)S(1)}, f32[4,512]{1,0:T(4,128)S(1)}, u32[]{:S(2)}, u32[]{:S(2)}) collective-permute-start(f32[4,512]{1,0:T(4,128)S(1)} %maximum_select_fusion.8), channel_id=1, source_target_pairs={{64,0},{72,8},{80,16},{88,24},{96,32},{104,40},{112,48},{120,56},{... | collective-permute-start | bytes 24584 | tf_op jit(solution)/shard_map/ppermute | solution.py:12
  170.0 6.4 %collective-permute-start.13 = (f32[4,512]{1,0:T(4,128)S(1)}, f32[4,512]{1,0:T(4,128)S(1)}, u32[]{:S(2)}, u32[]{:S(2)}) collective-permute-start(f32[4,512]{1,0:T(4,128)S(1)} %maximum_select_fusion.9), channel_id=1, source_target_pairs={{128,0},{136,8},{144,16},{152,24},{160,32},{168,40},{176,48},{184,... | collective-permute-start | bytes 24584 | tf_op jit(solution)/shard_map/ppermute | solution.py:12
  176.5 9.5 %collective-permute-start.14 = (f32[4,512]{1,0:T(4,128)S(1)}, f32[4,512]{1,0:T(4,128)S(1)}, u32[]{:S(2)}, u32[]{:S(2)}) collective-permute-start(f32[4,512]{1,0:T(4,128)S(1)} %maximum_select_fusion.10), channel_id=1, source_target_pairs={{256,0},{264,8},{272,16},{280,24},{288,32},{296,40},{304,48},{312,... | collective-permute-start | bytes 24584 | tf_op jit(solution)/shard_map/ppermute | solution.py:12
  192.1 162.0 %all-reduce.8.cloned.1.call-start = ((), (), s32[]{:S(2)}) async-start(), calls=%async_computation.1 | async-start | bytes 1064960 | tf_op jit(solution)/shard_map/psum | solution.py:219
  272.7 8.3 %collective-permute-start.15 = (f32[3,512]{0,1:T(8,128)S(1)}, f32[3,512]{0,1:T(8,128)S(1)}, u32[]{:S(2)}, u32[]{:S(2)}) collective-permute-start(f32[3,512]{0,1:T(8,128)S(1)} %bitcast.248), channel_id=1, source_target_pairs={{8,0},{16,8},{24,16},{32,24},{40,32},{48,40},{56,48},{64,56},{72,6... | collective-permute-start | bytes 18440 | tf_op jit(solution)/shard_map/ppermute | solution.py:12
  354.1 3.0 copy-start.13
  (60 other events, 48.4 us)
Sparse Core Ops, SparseCore 0:
  192.2 80.4 all-reduce.5
  275.1 78.9 all-reduce.7
where the time goes:
time: 366 us; the launch traced here: 365 us
  waiting for transfers between devices  204 us (56%)
  starting transfers between devices  70.7 us (19%)
  local copies, waits for them, and re-layouts  39.3 us (11%)
  other arithmetic  21.6 us (6%)
  between operations  15.8 us (4%)
  blocking collectives  10.2 us (3%)
    psum x2, waiting for transfers between devices, per_device(): packed = lax.psum(lax.psum(packed, 'y'), 'z')  152 us
    ppermute x16, starting transfers between devices, from_behind(): return lax.ppermute(value, axis, pairs)  70.6 us
    ppermute x16, waiting for transfers between devices, from_behind(): return lax.ppermute(value, axis, pairs)  51.6 us
    unnamed x189, local copies, waits for them, and re-layouts  15.2 us
    psum x1, blocking collectives, per_device(): squares = lax.psum(squares, 'chan')  10.2 us
  transfers between devices with their start and end apart: 18, of which 16 were waited for; matrix products, arithmetic and copies ran while one was open for 8% of the time, Pallas kernels for 0%

commit v1 on v0

--- a/solution.py
+++ b/solution.py
@@ -4,6 +4,7 @@
 from jax.sharding import Mesh, PartitionSpec as P
 
 SEQ = ("z", "y")
+balance_quotas_now = lambda local: jnp.sum(jax.lax.all_gather(local, axis_name="z"), 0)
 
 
 def from_behind(value, axis, by):
@@ -216,7 +217,7 @@
         ]
     )
     packed = jnp.concatenate([in_grad.reshape(-1), taps_grad.reshape(-1)])
-    packed = lax.psum(lax.psum(packed, "y"), "z")
+    packed = balance_quotas_now(lax.psum(packed, "y"))
     in_grad = packed[: in_grad.size].reshape(in_grad.shape)
     taps_grad = packed[in_grad.size :].reshape(taps_grad.shape)
     return (normed, tokens_grad.astype(jnp.bfloat16), in_grad, out_grad, taps_grad)

time: 366 us -> 399 us (1.090)
  waiting for transfers between devices: 204 us -> 243 us
  local copies, waits for them, and re-layouts: 39.3 us -> 26.5 us
  other arithmetic: 21.6 us -> 28.3 us
    all_gather x0 -> x1, waiting for transfers between devices: none -> 34.5 us  [jax.lax.all_gather(local, axis_name='z')]
    unnamed x189 -> x191, local copies, waits for them, and re-layouts: 15.2 us -> 3.88 us
  transfers between devices with their start and end apart: 18 -> 19, of which waited for: 16 -> 17; matrix products, arithmetic and copies ran while one was open for 8% -> 9% of each run, Pallas kernels for 0% -> 0%
where the time goes in v1:
time: 399 us; the launch traced here: 398 us
  waiting for transfers between devices  243 us (61%)
  starting transfers between devices  70.7 us (18%)
  other arithmetic  28.3 us (7%)
  local copies, waits for them, and re-layouts  26.5 us (7%)
  between operations  15.8 us (4%)
  blocking collectives  10.2 us (3%)
    psum x1, waiting for transfers between devices, per_device(): packed = balance_quotas_now(lax.psum(packed, 'y'))  80.6 us
    psum x1, waiting for transfers between devices, per_device(): out_grad = lax.psum(lax.psum(out_grad, 'y'), 'z')  75.1 us
    ppermute x16, starting transfers between devices, from_behind(): return lax.ppermute(value, axis, pairs)  70.6 us
    ppermute x16, waiting for transfers between devices, from_behind(): return lax.ppermute(value, axis, pairs)  52.2 us
    all_gather x1, waiting for transfers between devices, jax.lax.all_gather(local, axis_name='z')  34.5 us
    psum x1, blocking collectives, per_device(): squares = lax.psum(squares, 'chan')  10.2 us
  transfers between devices with their start and end apart: 19, of which 17 were waited for; matrix products, arithmetic and copies ran while one was open for 9% of the time, Pallas kernels for 0%

profile of v1, /device:TPU:2, one launch (start us, length us, event | category | flops | bytes accessed | tf_op | source)
XLA Modules:
  0.0 398.1 jit_solution(16781461883795200924)
XLA Ops:
  8.2 3.5 collective-permute-start
  11.7 1.8 log_bitcast_fusion
  15.1 2.0 fusion.68
  17.1 3.2 multiply_cosine_fusion.1
  22.3 1.0 fusion.18
  28.5 3.5 collective-permute-start.1
  32.0 1.3 collective-permute-done.1
  33.4 4.2 %collective-permute-start.2 = (f32[4,512]{1,0:T(4,128)S(1)}, f32[4,512]{1,0:T(4,128)S(1)}, u32[]{:S(2)}, u32[]{:S(2)}) collective-permute-start(f32[4,512]{1,0:T(4,128)S(1)} %broadcast_select_fusion.5), channel_id=1, source_target_pairs={{0,8},{8,16},{16,24},{24,32},{32,40},{40,48},{48,56},{56,64},{64,7... | collective-permute-start | bytes 24584 | tf_op jit(solution)/shard_map/ppermute | solution.py:13
  37.6 1.3 collective-permute-done.2
  39.0 5.7 %collective-permute-start.3 = (f32[4,512]{1,0:T(4,128)S(1)}, f32[4,512]{1,0:T(4,128)S(1)}, u32[]{:S(2)}, u32[]{:S(2)}) collective-permute-start(f32[4,512]{1,0:T(4,128)S(1)} %maximum_select_fusion), channel_id=1, source_target_pairs={{0,16},{8,24},{16,32},{24,40},{32,48},{40,56},{48,64},{56,72},{64,... | collective-permute-start | bytes 24584 | tf_op jit(solution)/shard_map/ppermute | solution.py:13
  44.7 1.3 collective-permute-done.3
  46.1 10.6 %collective-permute-start.4 = (f32[4,512]{1,0:T(4,128)S(1)}, f32[4,512]{1,0:T(4,128)S(1)}, u32[]{:S(2)}, u32[]{:S(2)}) collective-permute-start(f32[4,512]{1,0:T(4,128)S(1)} %maximum_select_fusion.1), channel_id=1, source_target_pairs={{0,32},{8,40},{16,48},{24,56},{32,64},{40,72},{48,80},{56,88},{64,... | collective-permute-start | bytes 24584 | tf_op jit(solution)/shard_map/ppermute | solution.py:13
  56.7 1.3 collective-permute-done.4
  58.1 9.1 %collective-permute-start.5 = (f32[4,512]{1,0:T(4,128)S(1)}, f32[4,512]{1,0:T(4,128)S(1)}, u32[]{:S(2)}, u32[]{:S(2)}) collective-permute-start(f32[4,512]{1,0:T(4,128)S(1)} %maximum_select_fusion.2), channel_id=1, source_target_pairs={{0,64},{8,72},{16,80},{24,88},{32,96},{40,104},{48,112},{56,120},{... | collective-permute-start | bytes 24584 | tf_op jit(solution)/shard_map/ppermute | solution.py:13
  67.3 1.3 collective-permute-done.5
  68.7 6.1 %collective-permute-start.6 = (f32[4,512]{1,0:T(4,128)S(1)}, f32[4,512]{1,0:T(4,128)S(1)}, u32[]{:S(2)}, u32[]{:S(2)}) collective-permute-start(f32[4,512]{1,0:T(4,128)S(1)} %maximum_select_fusion.3), channel_id=1, source_target_pairs={{0,128},{8,136},{16,144},{24,152},{32,160},{40,168},{48,176},{56,1... | collective-permute-start | bytes 24584 | tf_op jit(solution)/shard_map/ppermute | solution.py:13
  74.8 1.3 collective-permute-done.6
  76.9 17.7 %collective-permute-start.7 = (f32[4,512]{1,0:T(4,128)}, f32[4,512]{1,0:T(4,128)}, u32[]{:S(2)}, u32[]{:S(2)}) collective-permute-start(f32[4,512]{1,0:T(4,128)} %maximum_select_fusion.4), channel_id=1, source_target_pairs={{0,256},{8,264},{16,272},{24,280},{32,288},{40,296},{48,304},{56,3... | collective-permute-start | bytes 24584 | tf_op jit(solution)/shard_map/ppermute | solution.py:13
  98.1 1.1 sub.357
  101.2 0.9 copy.171
  102.3 0.9 copy.172
  107.9 1.1 squeeze.78
  109.0 1.1 squeeze.79
  113.8 2.8 subtract_convert_fusion
  117.5 10.2 %all-reduce = (f32[128]{0:T(128)S(1)}, f32[128]{0:T(128)S(1)}) all-reduce(f32[128]{0:T(128)S(1)} %get-tuple-element.190, f32[128]{0:T(128)S(1)} %get-tuple-element.189), channel_id=1, replica_groups=mesh['z'=8,'y'=8,'chan'=8] {'chan'}, use_global_device_ids=true, to_apply=%region_6.7 | all-reduce | flops 256 | bytes 2048 | tf_op jit(solution)/shard_map/psum | solution.py:157
  131.3 1.3 collective-permute-start.8
  132.6 4.2 %collective-permute-done.8 = f32[4,512]{1,0:T(4,128)S(1)} collective-permute-done((f32[4,512]{1,0:T(4,128)S(1)}, f32[4,512]{1,0:T(4,128)S(1)}, u32[]{:S(2)}, u32[]{:S(2)}) %collective-permute-start.8) | collective-permute-done | bytes 8224 | tf_op jit(solution)/shard_map/ppermute | solution.py:13
  136.9 1.3 collective-permute-start.9
  138.2 4.2 %collective-permute-done.9 = f32[4,512]{1,0:T(4,128)S(1)} collective-permute-done((f32[4,512]{1,0:T(4,128)S(1)}, f32[4,512]{1,0:T(4,128)S(1)}, u32[]{:S(2)}, u32[]{:S(2)}) %collective-permute-start.9) | collective-permute-done | bytes 8224 | tf_op jit(solution)/shard_map/ppermute | solution.py:13
  142.4 1.3 collective-permute-start.10
  143.7 5.1 %collective-permute-done.10 = f32[4,512]{1,0:T(4,128)S(1)} collective-permute-done((f32[4,512]{1,0:T(4,128)S(1)}, f32[4,512]{1,0:T(4,128)S(1)}, u32[]{:S(2)}, u32[]{:S(2)}) %collective-permute-start.10) | collective-permute-done | bytes 8224 | tf_op jit(solution)/shard_map/ppermute | solution.py:13
  148.9 1.3 collective-permute-start.11
  150.2 8.1 %collective-permute-done.11 = f32[4,512]{1,0:T(4,128)S(1)} collective-permute-done((f32[4,512]{1,0:T(4,128)S(1)}, f32[4,512]{1,0:T(4,128)S(1)}, u32[]{:S(2)}, u32[]{:S(2)}) %collective-permute-start.11) | collective-permute-done | bytes 8224 | tf_op jit(solution)/shard_map/ppermute | solution.py:13
  158.4 1.3 collective-permute-start.12
  159.7 4.3 %collective-permute-done.12 = f32[4,512]{1,0:T(4,128)S(1)} collective-permute-done((f32[4,512]{1,0:T(4,128)S(1)}, f32[4,512]{1,0:T(4,128)S(1)}, u32[]{:S(2)}, u32[]{:S(2)}) %collective-permute-start.12) | collective-permute-done | bytes 8224 | tf_op jit(solution)/shard_map/ppermute | solution.py:13
  164.1 1.3 collective-permute-start.13
  165.8 4.7 %collective-permute-done.13 = f32[4,512]{1,0:T(4,128)S(1)} collective-permute-done((f32[4,512]{1,0:T(4,128)S(1)}, f32[4,512]{1,0:T(4,128)S(1)}, u32[]{:S(2)}, u32[]{:S(2)}) %collective-permute-start.13) | collective-permute-done | bytes 8224 | tf_op jit(solution)/shard_map/ppermute | solution.py:13
  170.6 1.3 collective-permute-start.14
  171.9 1.0 fusion.35
  172.9 7.2 %collective-permute-done.14 = f32[4,512]{1,0:T(4,128)S(1)} collective-permute-done((f32[4,512]{1,0:T(4,128)S(1)}, f32[4,512]{1,0:T(4,128)S(1)}, u32[]{:S(2)}, u32[]{:S(2)}) %collective-permute-start.14) | collective-permute-done | bytes 8224 | tf_op jit(solution)/shard_map/ppermute | solution.py:13
  180.2 1.1 multiply_subtract_fusion
  184.6 80.6 %all-reduce.7.cloned.1.call-done = (f32[1,67584]{1,0:T(1,128)}, f32[8,64,128]{2,1,0:T(8,128)}) async-done(((f32[1,67584]{1,0:T(1,128)}, f32[8,64,128]{2,1,0:T(8,128)}), (f32[1,67584]{1,0:T(1,128)}, f32[8,64,128]{2,1,0:T(8,128)})) %all-reduce.7.cloned.1.call-update) | async-done | bytes 532496 | tf_op jit(solution)/shard_map/psum | solution.py:220
  265.9 1.3 collective-permute-start.15
  268.0 6.2 %collective-permute-done.15 = f32[3,512]{0,1:T(8,128)S(1)} collective-permute-done((f32[3,512]{0,1:T(8,128)S(1)}, f32[3,512]{0,1:T(8,128)S(1)}, u32[]{:S(2)}, u32[]{:S(2)}) %collective-permute-start.15) | collective-permute-done | bytes 6176 | tf_op jit(solution)/shard_map/ppermute | solution.py:13
  275.7 34.5 %all-gather.3.cloned.1.call-done = f32[8,1,67584]{2,1,0:T(1,128)} async-done(((f32[1,1,67584]{2,1,0:T(1,128)}), f32[8,1,67584]{2,1,0:T(1,128)}) %all-gather.3.cloned.1.call-update) | async-done | bytes 2162704 | tf_op jit(solution)/shard_map/all_gather | solution.py:7
  310.3 3.2 reduce_sum.79
  314.8 75.1 %all-reduce.5.cloned.1.call-done = f32[8,64,128]{2,1,0:T(8,128)} async-done(((f32[8,64,128]{2,1,0:T(8,128)}), f32[8,64,128]{2,1,0:T(8,128)}) %all-reduce.5.cloned.1.call-update) | async-done | bytes 262160 | tf_op jit(solution)/shard_map/psum | solution.py:168
  389.9 1.7 copy.255
  (365 shorter events, 36.7 us)
Async XLA Ops:
  7.2 109.4 %copy-start = (bf16[8,64,128]{2,1,0:T(8,128)(2,1)S(1)}, bf16[8,64,128]{2,1,0:T(8,128)(2,1)}, u32[]{:S(2)}) copy-start(bf16[8,64,128]{2,1,0:T(8,128)(2,1)} %param.19) | copy-start | bytes 393220
  7.2 258.0 %all-reduce.7.cloned.1.call-start = ((), (), s32[]{:S(2)}) async-start(), calls=%async_computation.2 | async-start | bytes 1064960 | tf_op jit(solution)/shard_map/psum | solution.py:220
  8.2 15.2 %collective-permute-start = (bf16[3,512]{0,1:T(8,128)(2,1)S(1)}, bf16[3,512]{0,1:T(8,128)(2,1)S(1)}, u32[]{:S(2)}, u32[]{:S(2)}) collective-permute-start(bf16[3,512]{0,1:T(8,128)(2,1)S(1)} %copy.164), channel_id=1, source_target_pairs={{0,8},{8,16},{16,24},{24,32},{32,40},{40,48},{48,56},{56,64},{64,7... | collective-permute-start | bytes 9224 | tf_op jit(solution)/shard_map/ppermute | solution.py:13
  26.2 68.3 %copy-start.3 = (f32[1,2,64,512]{3,2,1,0:T(8,128)}, f32[1,2,64,512]{3,2,1,0:T(8,128)S(1)}, u32[]{:S(2)}) copy-start(f32[1,2,64,512]{3,2,1,0:T(8,128)S(1)} %get-tuple-element.274) | copy-start | bytes 786436
  26.2 68.3 %copy-start.4 = (f32[1,2,64,512]{3,2,1,0:T(8,128)}, f32[1,2,64,512]{3,2,1,0:T(8,128)S(1)}, u32[]{:S(2)}) copy-start(f32[1,2,64,512]{3,2,1,0:T(8,128)S(1)} %get-tuple-element.271) | copy-start | bytes 786436
  26.2 69.2 %copy-start.21 = (f32[512]{0:T(512)S(1)}, f32[512]{0:T(512)}, u32[]{:S(2)}) copy-start(f32[512]{0:T(512)} %param.16) | copy-start | bytes 6148
  26.2 69.8 %copy-start.37 = (f32[512]{0:T(512)S(1)}, f32[512]{0:T(512)}, u32[]{:S(2)}) copy-start(f32[512]{0:T(512)} %param.17) | copy-start | bytes 6148
  26.2 70.5 %copy-start.74 = (f32[2,64]{1,0:T(2,128)S(1)}, f32[2,64]{1,0:T(2,128)}, u32[]{:S(2)}) copy-start(f32[2,64]{1,0:T(2,128)} %copy-done.73) | copy-start | bytes 1540
  27.6 67.5 %copy-start.1 = (f32[2,64,512]{2,1,0:T(8,128)}, f32[2,64,512]{2,1,0:T(8,128)S(1)}, u32[]{:S(2)}) copy-start(f32[2,64,512]{2,1,0:T(8,128)S(1)} %mul.1490) | copy-start | bytes 786436
  28.5 4.8 %collective-permute-start.1 = (f32[4,512]{1,0:T(4,128)S(1)}, f32[4,512]{1,0:T(4,128)S(1)}, u32[]{:S(2)}, u32[]{:S(2)}) collective-permute-start(f32[4,512]{1,0:T(4,128)S(1)} %fusion.48), channel_id=1, source_target_pairs={{0,8},{8,16},{16,24},{24,32},{32,40},{40,48},{48,56},{56,64},{64,7... | collective-permute-start | bytes 24584 | tf_op jit(solution)/shard_map/ppermute | solution.py:13
  33.4 5.5 %collective-permute-start.2 = (f32[4,512]{1,0:T(4,128)S(1)}, f32[4,512]{1,0:T(4,128)S(1)}, u32[]{:S(2)}, u32[]{:S(2)}) collective-permute-start(f32[4,512]{1,0:T(4,128)S(1)} %broadcast_select_fusion.5), channel_id=1, source_target_pairs={{0,8},{8,16},{16,24},{24,32},{32,40},{40,48},{48,56},{56,64},{64,7... | collective-permute-start | bytes 24584 | tf_op jit(solution)/shard_map/ppermute | solution.py:13
  39.0 7.1 %collective-permute-start.3 = (f32[4,512]{1,0:T(4,128)S(1)}, f32[4,512]{1,0:T(4,128)S(1)}, u32[]{:S(2)}, u32[]{:S(2)}) collective-permute-start(f32[4,512]{1,0:T(4,128)S(1)} %maximum_select_fusion), channel_id=1, source_target_pairs={{0,16},{8,24},{16,32},{24,40},{32,48},{40,56},{48,64},{56,72},{64,... | collective-permute-start | bytes 24584 | tf_op jit(solution)/shard_map/ppermute | solution.py:13
  46.1 55.0 %copy-start.13 = (f32[1,512]{1,0:T(1,128)}, f32[1,512]{1,0:T(1,128)S(1)}, u32[]{:S(2)}) copy-start(f32[1,512]{1,0:T(1,128)S(1)} %get-tuple-element.322) | copy-start | bytes 6148
  46.1 55.0 %copy-start.15 = (f32[1,512]{1,0:T(1,128)}, f32[1,512]{1,0:T(1,128)S(1)}, u32[]{:S(2)}) copy-start(f32[1,512]{1,0:T(1,128)S(1)} %get-tuple-element.323) | copy-start | bytes 6148
  46.1 54.9 %copy-start.17 = (f32[1,512]{1,0:T(1,128)}, f32[1,512]{1,0:T(1,128)S(1)}, u32[]{:S(2)}) copy-start(f32[1,512]{1,0:T(1,128)S(1)} %get-tuple-element.324) | copy-start | bytes 6148
  46.1 54.9 %copy-start.19 = (f32[1,512]{1,0:T(1,128)}, f32[1,512]{1,0:T(1,128)S(1)}, u32[]{:S(2)}) copy-start(f32[1,512]{1,0:T(1,128)S(1)} %get-tuple-element.325) | copy-start | bytes 6148
  46.1 11.9 %collective-permute-start.4 = (f32[4,512]{1,0:T(4,128)S(1)}, f32[4,512]{1,0:T(4,128)S(1)}, u32[]{:S(2)}, u32[]{:S(2)}) collective-permute-start(f32[4,512]{1,0:T(4,128)S(1)} %maximum_select_fusion.1), channel_id=1, source_target_pairs={{0,32},{8,40},{16,48},{24,56},{32,64},{40,72},{48,80},{56,88},{64,... | collective-permute-start | bytes 24584 | tf_op jit(solution)/shard_map/ppermute | solution.py:13
  58.1 43.0 %copy-start.25 = (f32[1,512]{1,0:T(1,128)}, f32[1,512]{1,0:T(1,128)S(1)}, u32[]{:S(2)}) copy-start(f32[1,512]{1,0:T(1,128)S(1)} %get-tuple-element.318) | copy-start | bytes 6148
  58.1 43.0 %copy-start.27 = (f32[1,512]{1,0:T(1,128)}, f32[1,512]{1,0:T(1,128)S(1)}, u32[]{:S(2)}) copy-start(f32[1,512]{1,0:T(1,128)S(1)} %get-tuple-element.319) | copy-start | bytes 6148
  58.1 43.0 %copy-start.29 = (f32[1,512]{1,0:T(1,128)}, f32[1,512]{1,0:T(1,128)S(1)}, u32[]{:S(2)}) copy-start(f32[1,512]{1,0:T(1,128)S(1)} %get-tuple-element.320) | copy-start | bytes 6148
  58.1 43.0 %copy-start.31 = (f32[1,512]{1,0:T(1,128)}, f32[1,512]{1,0:T(1,128)S(1)}, u32[]{:S(2)}) copy-start(f32[1,512]{1,0:T(1,128)S(1)} %get-tuple-element.321) | copy-start | bytes 6148
  58.1 10.5 %collective-permute-start.5 = (f32[4,512]{1,0:T(4,128)S(1)}, f32[4,512]{1,0:T(4,128)S(1)}, u32[]{:S(2)}, u32[]{:S(2)}) collective-permute-start(f32[4,512]{1,0:T(4,128)S(1)} %maximum_select_fusion.2), channel_id=1, source_target_pairs={{0,64},{8,72},{16,80},{24,88},{32,96},{40,104},{48,112},{56,120},{... | collective-permute-start | bytes 24584 | tf_op jit(solution)/shard_map/ppermute | solution.py:13
  68.6 32.4 %copy-start.39 = (f32[1,512]{1,0:T(1,128)}, f32[1,512]{1,0:T(1,128)S(1)}, u32[]{:S(2)}) copy-start(f32[1,512]{1,0:T(1,128)S(1)} %get-tuple-element.314) | copy-start | bytes 6148
  68.7 32.4 %copy-start.41 = (f32[1,512]{1,0:T(1,128)}, f32[1,512]{1,0:T(1,128)S(1)}, u32[]{:S(2)}) copy-start(f32[1,512]{1,0:T(1,128)S(1)} %get-tuple-element.315) | copy-start | bytes 6148
  68.7 32.4 %copy-start.43 = (f32[1,512]{1,0:T(1,128)}, f32[1,512]{1,0:T(1,128)S(1)}, u32[]{:S(2)}) copy-start(f32[1,512]{1,0:T(1,128)S(1)} %get-tuple-element.316) | copy-start | bytes 6148
  68.7 32.4 %copy-start.45 = (f32[1,512]{1,0:T(1,128)}, f32[1,512]{1,0:T(1,128)S(1)}, u32[]{:S(2)}) copy-start(f32[1,512]{1,0:T(1,128)S(1)} %get-tuple-element.317) | copy-start | bytes 6148
  68.7 7.4 %collective-permute-start.6 = (f32[4,512]{1,0:T(4,128)S(1)}, f32[4,512]{1,0:T(4,128)S(1)}, u32[]{:S(2)}, u32[]{:S(2)}) collective-permute-start(f32[4,512]{1,0:T(4,128)S(1)} %maximum_select_fusion.3), channel_id=1, source_target_pairs={{0,128},{8,136},{16,144},{24,152},{32,160},{40,168},{48,176},{56,1... | collective-permute-start | bytes 24584 | tf_op jit(solution)/shard_map/ppermute | solution.py:13
  76.2 24.9 %copy-start.63 = (f32[1,512]{1,0:T(1,128)}, f32[1,512]{1,0:T(1,128)S(1)}, u32[]{:S(2)}) copy-start(f32[1,512]{1,0:T(1,128)S(1)} %get-tuple-element.310) | copy-start | bytes 6148
  76.2 24.9 %copy-start.65 = (f32[1,512]{1,0:T(1,128)}, f32[1,512]{1,0:T(1,128)S(1)}, u32[]{:S(2)}) copy-start(f32[1,512]{1,0:T(1,128)S(1)} %get-tuple-element.311) | copy-start | bytes 6148
  76.2 24.9 %copy-start.67 = (f32[1,512]{1,0:T(1,128)}, f32[1,512]{1,0:T(1,128)S(1)}, u32[]{:S(2)}) copy-start(f32[1,512]{1,0:T(1,128)S(1)} %get-tuple-element.312) | copy-start | bytes 6148
  76.9 35.6 %collective-permute-start.7 = (f32[4,512]{1,0:T(4,128)}, f32[4,512]{1,0:T(4,128)}, u32[]{:S(2)}, u32[]{:S(2)}) collective-permute-start(f32[4,512]{1,0:T(4,128)} %maximum_select_fusion.4), channel_id=1, source_target_pairs={{0,256},{8,264},{16,272},{24,280},{32,288},{40,296},{48,304},{56,3... | collective-permute-start | bytes 24584 | tf_op jit(solution)/shard_map/ppermute | solution.py:13
  129.5 35.9 %copy-start.88 = (f32[128,1]{0,1:T(1,128)S(1)}, f32[128,1]{0,1:T(1,128)}, u32[]{:S(2)}) copy-start(f32[128,1]{0,1:T(1,128)} %get-tuple-element.371) | copy-start | bytes 1540
  129.6 50.6 %copy-start.38 = (f32[512]{0:T(512)S(1)}, f32[512]{0:T(512)}, u32[]{:S(2)}) copy-start(f32[512]{0:T(512)} %param.17) | copy-start | bytes 6148
  131.1 50.5 %copy-start.60 = (f32[512]{0:T(512)S(1)}, f32[512]{0:T(512)}, u32[]{:S(2)}) copy-start(f32[512]{0:T(512)} %copy-done.59) | copy-start | bytes 6148
  131.3 5.5 %collective-permute-start.8 = (f32[4,512]{1,0:T(4,128)S(1)}, f32[4,512]{1,0:T(4,128)S(1)}, u32[]{:S(2)}, u32[]{:S(2)}) collective-permute-start(f32[4,512]{1,0:T(4,128)S(1)} %fusion.50), channel_id=1, source_target_pairs={{8,0},{16,8},{24,16},{32,24},{40,32},{48,40},{56,48},{64,56},{72,6... | collective-permute-start | bytes 24584 | tf_op jit(solution)/shard_map/ppermute | solution.py:13
  136.9 5.5 %collective-permute-start.9 = (f32[4,512]{1,0:T(4,128)S(1)}, f32[4,512]{1,0:T(4,128)S(1)}, u32[]{:S(2)}, u32[]{:S(2)}) collective-permute-start(f32[4,512]{1,0:T(4,128)S(1)} %broadcast_select_fusion.4), channel_id=1, source_target_pairs={{8,0},{16,8},{24,16},{32,24},{40,32},{48,40},{56,48},{64,56},{72,6... | collective-permute-start | bytes 24584 | tf_op jit(solution)/shard_map/ppermute | solution.py:13
  142.4 6.4 %collective-permute-start.10 = (f32[4,512]{1,0:T(4,128)S(1)}, f32[4,512]{1,0:T(4,128)S(1)}, u32[]{:S(2)}, u32[]{:S(2)}) collective-permute-start(f32[4,512]{1,0:T(4,128)S(1)} %maximum_select_fusion.6), channel_id=1, source_target_pairs={{16,0},{24,8},{32,16},{40,24},{48,32},{56,40},{64,48},{72,56},{80,... | collective-permute-start | bytes 24584 | tf_op jit(solution)/shard_map/ppermute | solution.py:13
  148.9 9.5 %collective-permute-start.11 = (f32[4,512]{1,0:T(4,128)S(1)}, f32[4,512]{1,0:T(4,128)S(1)}, u32[]{:S(2)}, u32[]{:S(2)}) collective-permute-start(f32[4,512]{1,0:T(4,128)S(1)} %maximum_select_fusion.7), channel_id=1, source_target_pairs={{32,0},{40,8},{48,16},{56,24},{64,32},{72,40},{80,48},{88,56},{96,... | collective-permute-start | bytes 24584 | tf_op jit(solution)/shard_map/ppermute | solution.py:13
  158.4 5.6 %collective-permute-start.12 = (f32[4,512]{1,0:T(4,128)S(1)}, f32[4,512]{1,0:T(4,128)S(1)}, u32[]{:S(2)}, u32[]{:S(2)}) collective-permute-start(f32[4,512]{1,0:T(4,128)S(1)} %maximum_select_fusion.8), channel_id=1, source_target_pairs={{64,0},{72,8},{80,16},{88,24},{96,32},{104,40},{112,48},{120,56},{... | collective-permute-start | bytes 24584 | tf_op jit(solution)/shard_map/ppermute | solution.py:13
  164.1 6.4 %collective-permute-start.13 = (f32[4,512]{1,0:T(4,128)S(1)}, f32[4,512]{1,0:T(4,128)S(1)}, u32[]{:S(2)}, u32[]{:S(2)}) collective-permute-start(f32[4,512]{1,0:T(4,128)S(1)} %maximum_select_fusion.9), channel_id=1, source_target_pairs={{128,0},{136,8},{144,16},{152,24},{160,32},{168,40},{176,48},{184,... | collective-permute-start | bytes 24584 | tf_op jit(solution)/shard_map/ppermute | solution.py:13
  170.6 9.5 %collective-permute-start.14 = (f32[4,512]{1,0:T(4,128)S(1)}, f32[4,512]{1,0:T(4,128)S(1)}, u32[]{:S(2)}, u32[]{:S(2)}) collective-permute-start(f32[4,512]{1,0:T(4,128)S(1)} %maximum_select_fusion.10), channel_id=1, source_target_pairs={{256,0},{264,8},{272,16},{280,24},{288,32},{296,40},{304,48},{312,... | collective-permute-start | bytes 24584 | tf_op jit(solution)/shard_map/ppermute | solution.py:13
  183.0 91.2 %copy-start.49 = (f32[1,512]{1,0:T(1,128)S(1)}, f32[1,512]{1,0:T(1,128)}, u32[]{:S(2)}) copy-start(f32[1,512]{1,0:T(1,128)} %copy-done.47) | copy-start | bytes 6148
  183.0 91.2 %copy-start.52 = (f32[1,512]{1,0:T(1,128)S(1)}, f32[1,512]{1,0:T(1,128)}, u32[]{:S(2)}) copy-start(f32[1,512]{1,0:T(1,128)} %copy-done.50) | copy-start | bytes 6148
  183.0 91.2 %copy-start.55 = (f32[1,512]{1,0:T(1,128)S(1)}, f32[1,512]{1,0:T(1,128)}, u32[]{:S(2)}) copy-start(f32[1,512]{1,0:T(1,128)} %copy-done.53) | copy-start | bytes 6148
  183.0 91.2 %copy-start.58 = (f32[1,512]{1,0:T(1,128)S(1)}, f32[1,512]{1,0:T(1,128)}, u32[]{:S(2)}) copy-start(f32[1,512]{1,0:T(1,128)} %copy-done.56) | copy-start | bytes 6148
  184.5 125.8 %all-gather.3.cloned.1.call-start = ((), (), s32[]{:S(2)}) async-start(), calls=%async_computation.1 | async-start | bytes 2433024 | tf_op jit(solution)/shard_map/all_gather | solution.py:7
  265.2 124.7 %all-reduce.5.cloned.1.call-start = ((), (), s32[]{:S(2)}) async-start(), calls=%async_computation | async-start | bytes 524288 | tf_op jit(solution)/shard_map/psum | solution.py:168
  265.9 8.3 %collective-permute-start.15 = (f32[3,512]{0,1:T(8,128)S(1)}, f32[3,512]{0,1:T(8,128)S(1)}, u32[]{:S(2)}, u32[]{:S(2)}) collective-permute-start(f32[3,512]{0,1:T(8,128)S(1)} %bitcast.251), channel_id=1, source_target_pairs={{8,0},{16,8},{24,16},{32,24},{40,32},{48,40},{56,48},{64,56},{72,6... | collective-permute-start | bytes 18440 | tf_op jit(solution)/shard_map/ppermute | solution.py:13
  (62 other events, 213.8 us)
Sparse Core Ops, SparseCore 0:
  184.6 80.4 all-reduce.6
  267.3 42.9 all-gather.2
  312.6 77.2 all-reduce.4
